TPU v7x, 512 devices: a whole 4x4x16 slice. The times are simulated.
512 devices in a mesh: fibre: 32 (over z, core), group: 16 (over y, x).
Axes of the slice: x: 4, y: 4, z: 16, core: 2. Of those that a mesh axis runs over, the one named last changes fastest.
Arguments:
- species_field: float32 [512, 524288], P('fibre', 'group'), may hold values from -45 to 45, as said below
- start_block: float32 [512, 64], replicated, may hold values from -4 to 4
Outputs:
- mode_basis: float32 [512, 64], replicated
- core_tensor: float32 [64, 524288], P(None, ('group', 'fibre'))
Inputs may be any that keep to these rules, and one draw needn't show every extreme that they name: `species_field`: float32 field values.
All inputs are finite; a program needn't handle non-finite values.
Results may differ from a plain program's by a relative error of at most 0.0003.
Values sent between devices are 32-bit elements; how exact they have to be, the bound alone decides.
No kernel may reach another device: no remote copies, remote signals or barrier semaphores. Data moves between devices by JAX's collectives and lax.ppermute only.
A program may use at most 64 MiB of HBM per device.

v0:
```python
import jax
import jax.numpy as jnp
from jax import lax
from jax.sharding import PartitionSpec as P

ITERS = 3
highest_precision = lax.Precision.HIGHEST


def orthonormal(matrix):
    inner_gram = jnp.dot(matrix.T, matrix, precision=highest_precision)
    lower_factor = jnp.linalg.cholesky(inner_gram)
    return lax.linalg.triangular_solve(
        lower_factor, matrix, left_side=False, lower=True, transpose_a=True
    )


def on_device(species_field, start_block):
    fibres = lax.all_to_all(species_field, "fibre", split_axis=1, concat_axis=0, tiled=True)
    total_columns = fibres.shape[1] * lax.axis_size("fibre") * lax.axis_size("group")
    mode_basis = orthonormal(start_block)
    local_gram = jnp.dot(fibres, fibres.T, precision=highest_precision) / total_columns
    gram_matrix = lax.psum(local_gram, ("fibre", "group"))
    for iteration in range(ITERS):
        mode_basis = orthonormal(jnp.dot(gram_matrix, mode_basis, precision=highest_precision))
    core_tensor = jnp.dot(mode_basis.T, fibres, precision=highest_precision)
    return (mode_basis, core_tensor)


def solution(mesh):
    placed = (P("fibre", "group"), P())
    return jax.shard_map(
        on_device,
        mesh=mesh,
        in_specs=placed,
        out_specs=(P(), P(None, ("group", "fibre"))),
        check_vma=False,
    )
```

profile of v0, /device:TPU:1, one launch (start us, length us, event | category | flops | bytes accessed | tf_op | source)
XLA Modules:
  0.0 643.5 jit_solution(7276870236529994059)
XLA Ops:
  7.2 0.0 copy-start
  7.2 3.2 copy.24
  10.4 16.7 %all-to-all-start = ((f32[16,32,1024]{2,0,1:T(8,128)}), f32[16,32,1024]{2,0,1:T(8,128)S(1)}, u32[]{:S(2)}, u32[]{:S(2)}) async-start(f32[16,32,1024]{2,0,1:T(8,128)} %bitcast.75), calls=%async_computation | async-start | bytes 4194304 | tf_op jit(solution)/shard_map/all_to_all | solution.py:19
  27.2 0.0 all-reduce.2.cloned.1.call-start
  27.2 0.0 copy-done
  27.2 0.3 fusion.18
  27.5 0.1 copy.18
  27.6 5.8 cholesky.74
  33.5 92.3 %all-to-all-done = f32[16,32,1024]{2,0,1:T(8,128)S(1)} async-done(((f32[16,32,1024]{2,0,1:T(8,128)}), f32[16,32,1024]{2,0,1:T(8,128)S(1)}, u32[]{:S(2)}, u32[]{:S(2)}) %all-to-all-start) | async-done | bytes 2097184 | tf_op jit(solution)/shard_map/all_to_all | solution.py:19
  125.8 4.6 convolution_multiply_fusion
  130.3 0.0 all-reduce.2.cloned.1.call-update
  130.4 0.6 compare_reduce_fusion.3
  131.0 0.7 fusion
  131.6 4.9 custom-call.8
  136.5 0.3 convolution_bitcast_fusion.3
  136.9 454.4 %all-reduce.2.cloned.1.call-done = f32[512,512]{1,0:T(8,128)} async-done(((f32[512,512]{1,0:T(8,128)}), f32[512,512]{1,0:T(8,128)}) %all-reduce.2.cloned.1.call-update) | async-done | bytes 1048592 | tf_op jit(solution)/shard_map/psum | solution.py:23
  591.3 0.0 copy-start.1
  591.3 2.4 fusion.19
  593.7 0.3 fusion.20
  594.0 0.1 copy.19
  594.1 5.8 cholesky.85
  600.0 0.6 compare_reduce_fusion.2
  600.6 0.7 fusion.1
  601.3 4.9 custom-call.9
  606.2 0.3 convolution_bitcast_fusion.2
  606.5 0.0 copy-done.1
  606.5 1.1 fusion.21
  607.6 0.3 fusion.22
  607.9 0.1 copy.20
  608.0 5.8 cholesky.96
  613.9 0.6 compare_reduce_fusion.1
  614.5 0.7 fusion.2
  615.2 4.9 custom-call.10
  620.1 0.3 convolution_bitcast_fusion.1
  620.4 1.3 fusion.23
  621.8 0.3 fusion.24
  622.0 0.1 copy.21
  622.1 5.8 cholesky.107
  628.0 0.6 compare_reduce_fusion
  628.6 0.7 fusion.3
  629.3 4.9 custom-call.11
  634.2 0.3 convolution_bitcast_fusion
  634.5 0.0 copy-start.2
  634.6 2.1 fusion.25
  636.6 0.0 copy-done.2
  (8 shorter events, 0.2 us)
Async XLA Ops:
  7.2 20.0 %copy-start = (f32[512,64]{0,1:T(8,128)S(1)}, f32[512,64]{0,1:T(8,128)}, u32[]{:S(2)}) copy-start(f32[512,64]{0,1:T(8,128)} %param.6) | copy-start | bytes 393220
  10.4 115.4 %all-to-all-start = ((f32[16,32,1024]{2,0,1:T(8,128)}), f32[16,32,1024]{2,0,1:T(8,128)S(1)}, u32[]{:S(2)}, u32[]{:S(2)}) async-start(f32[16,32,1024]{2,0,1:T(8,128)} %bitcast.75), calls=%async_computation | async-start | bytes 4194304 | tf_op jit(solution)/shard_map/all_to_all | solution.py:19
  27.2 564.1 %all-reduce.2.cloned.1.call-start = ((), (), s32[]{:S(2)}) async-start(), calls=%async_computation.1 | async-start | bytes 2097152 | tf_op jit(solution)/shard_map/psum | solution.py:23
  591.3 15.2 %copy-start.1 = (f32[512,512]{1,0:T(8,128)S(1)}, f32[512,512]{1,0:T(8,128)}, u32[]{:S(2)}) copy-start(f32[512,512]{1,0:T(8,128)} %all-reduce.2.cloned.1.call-done) | copy-start | bytes 3145732
  634.5 2.1 copy-start.2
Sparse Core Ops, SparseCore 0:
  130.5 460.7 all-reduce.1
where the time goes:
time: 644 us; the launch traced here: 643 us
  waiting for transfers between devices  547 us (85%)
  other arithmetic  48.3 us (8%)
  starting transfers between devices  16.8 us (3%)
  between operations  14.2 us (2%)
  matrix products  13.9 us (2%)
    psum x1, waiting for transfers between devices, on_device(): gram_matrix = lax.psum(local_gram, ('fibre', 'group'))  454 us
    all_to_all x1, waiting for transfers between devices, on_device(): lax.all_to_all(species_field, 'fibre', split_axis=1, concat_axis=0, tiled...  92.3 us
    another operation x12, other arithmetic, orthonormal(): lower_factor = jnp.linalg.cholesky(inner_gram)  26.1 us
    another operation x8, other arithmetic, orthonormal(): lax.linalg.triangular_solve(lower_factor, matrix, left_side=False, lower=...  22.2 us
    all_to_all x1, starting transfers between devices, on_device(): lax.all_to_all(species_field, 'fibre', split_axis=1, concat_axis=0, tiled...  16.7 us
  transfers between devices with their start and end apart: 2, of which 2 were waited for; matrix products, arithmetic and copies ran while one was open for 2% of the time, Pallas kernels for 0%

commit v1 on v0

--- a/solution.py
+++ b/solution.py
@@ -2,6 +2,7 @@
 import jax.numpy as jnp
 from jax import lax
 from jax.sharding import PartitionSpec as P
+from jax.lax import psum
 
 ITERS = 3
 highest_precision = lax.Precision.HIGHEST
@@ -20,7 +21,12 @@
     total_columns = fibres.shape[1] * lax.axis_size("fibre") * lax.axis_size("group")
     mode_basis = orthonormal(start_block)
     local_gram = jnp.dot(fibres, fibres.T, precision=highest_precision) / total_columns
-    gram_matrix = lax.psum(local_gram, ("fibre", "group"))
+
+    def put_run(x_local):
+        wide_out = psum(x_local, "fibre")
+        return psum(wide_out, "group")
+
+    gram_matrix = put_run(local_gram)
     for iteration in range(ITERS):
         mode_basis = orthonormal(jnp.dot(gram_matrix, mode_basis, precision=highest_precision))
     core_tensor = jnp.dot(mode_basis.T, fibres, precision=highest_precision)

time: 644 us -> 505 us (0.78)
  waiting for transfers between devices: 547 us -> 309 us
  blocking collectives: 0 us -> 117 us
  starting transfers between devices: 16.8 us -> 0.26 us
    psum x1 -> x2, waiting for transfers between devices: 454 us -> 309 us  [the longest x1 202 us: put_run(): wide_out = psum(x_local, 'fibre')]
    all_to_all x0 -> x1, blocking collectives: none -> 117 us  [on_device(): lax.all_to_all(species_field, 'fibre', split_axis=1, concat_axis=0, tiled...]
    all_to_all x1 -> x0, waiting for transfers between devices: 92.3 us -> none  [on_device(): lax.all_to_all(species_field, 'fibre', split_axis=1, concat_axis=0, tiled...]
    all_to_all x1 -> x0, starting transfers between devices: 16.7 us -> none  [on_device(): lax.all_to_all(species_field, 'fibre', split_axis=1, concat_axis=0, tiled...]
  transfers between devices with their start and end apart: 2 -> 2, of which waited for: 2 -> 2; matrix products, arithmetic and copies ran while one was open for 2% -> 3% of each run, Pallas kernels for 0% -> 0%
where the time goes in v1:
time: 505 us
  waiting for transfers between devices  309 us (61%)
  blocking collectives  117 us (23%)
  other arithmetic  48.3 us (10%)
  between operations  14.2 us (3%)
  matrix products  13.8 us (3%)
    psum x1, waiting for transfers between devices, put_run(): wide_out = psum(x_local, 'fibre')  202 us
    all_to_all x1, blocking collectives, on_device(): lax.all_to_all(species_field, 'fibre', split_axis=1, concat_axis=0, tiled...  117 us
    psum x1, waiting for transfers between devices, put_run(): return psum(wide_out, 'group')  107 us
    another operation x12, other arithmetic, orthonormal(): lower_factor = jnp.linalg.cholesky(inner_gram)  26.1 us
    another operation x8, other arithmetic, orthonormal(): lax.linalg.triangular_solve(lower_factor, matrix, left_side=False, lower=...  22.2 us
  transfers between devices with their start and end apart: 2, of which 2 were waited for; matrix products, arithmetic and copies ran while one was open for 3% of the time, Pallas kernels for 0%

profile of v1, /device:TPU:1, one launch (start us, length us, event | category | flops | bytes accessed | tf_op | source)
XLA Modules:
  0.0 504.5 jit_solution(4016844151795974575)
XLA Ops:
  7.2 0.0 copy-start
  7.2 0.0 all-reduce.3.cloned.1.call-start
  7.2 1.8 copy.24
  9.0 117.2 %all_to_all.19 = f32[16,32,1024]{2,0,1:T(8,128)S(1)} all-to-all(f32[16,32,1024]{2,0,1:T(8,128)S(1)} %bitcast.75), channel_id=1, replica_groups=mesh['fibre'=32,'group'=16] {'fibre'}, dimensions={1} | all-to-all | bytes 4194304 | tf_op jit(solution)/shard_map/all_to_all | solution.py:20
  126.2 4.6 convolution_multiply_fusion
  130.8 0.0 all-reduce.3.cloned.1.call-update
  130.8 0.2 all-reduce.5.cloned.1.call-start
  131.0 201.8 %all-reduce.3.cloned.1.call-done = f32[512,512]{1,0:T(8,128)} async-done(((f32[512,512]{1,0:T(8,128)}), f32[512,512]{1,0:T(8,128)}) %all-reduce.3.cloned.1.call-update) | async-done | bytes 1048592 | tf_op jit(solution)/shard_map/psum | solution.py:26
  332.8 0.0 all-reduce.5.cloned.1.call-update
  332.8 0.0 copy-done
  332.8 0.3 fusion.18
  333.1 0.1 copy.18
  333.2 5.8 %cholesky.74 = f32[64,64]{1,0:T(8,128)S(1)} custom-call(f32[64,64]{1,0:T(8,128)S(1)} %fusion.11), custom_call_target="Cholesky" | custom-call | tf_op jit(solution)/shard_map/jit(cholesky)/cholesky | solution.py:13
  339.1 0.6 compare_reduce_fusion.3
  339.7 0.7 fusion
  340.4 4.9 custom-call.8
  345.3 0.3 convolution_bitcast_fusion.3
  345.6 106.9 %all-reduce.5.cloned.1.call-done = f32[512,512]{1,0:T(8,128)} async-done(((f32[512,512]{1,0:T(8,128)}), f32[512,512]{1,0:T(8,128)}) %all-reduce.5.cloned.1.call-update) | async-done | bytes 1048592 | tf_op jit(solution)/shard_map/psum | solution.py:27
  452.5 0.0 copy-start.1
  452.5 2.4 fusion.19
  454.9 0.3 fusion.20
  455.2 0.1 copy.19
  455.3 5.8 %cholesky.85 = f32[64,64]{1,0:T(8,128)S(1)} custom-call(f32[64,64]{1,0:T(8,128)S(1)} %fusion.9), custom_call_target="Cholesky" | custom-call | tf_op jit(solution)/shard_map/jit(cholesky)/cholesky | solution.py:13
  461.2 0.6 compare_reduce_fusion.2
  461.8 0.7 fusion.1
  462.5 4.9 custom-call.9
  467.4 0.3 convolution_bitcast_fusion.2
  467.7 0.0 copy-done.1
  467.7 1.1 fusion.21
  468.9 0.3 fusion.22
  469.1 0.1 copy.20
  469.2 5.8 %cholesky.96 = f32[64,64]{1,0:T(8,128)S(1)} custom-call(f32[64,64]{1,0:T(8,128)S(1)} %fusion.7), custom_call_target="Cholesky" | custom-call | tf_op jit(solution)/shard_map/jit(cholesky)/cholesky | solution.py:13
  475.1 0.6 compare_reduce_fusion.1
  475.8 0.7 fusion.2
  476.4 4.9 custom-call.10
  481.3 0.3 convolution_bitcast_fusion.1
  481.7 1.1 fusion.23
  482.8 0.3 fusion.24
  483.1 0.1 copy.21
  483.2 5.8 %cholesky.107 = f32[64,64]{1,0:T(8,128)S(1)} custom-call(f32[64,64]{1,0:T(8,128)S(1)} %fusion.5), custom_call_target="Cholesky" | custom-call | tf_op jit(solution)/shard_map/jit(cholesky)/cholesky | solution.py:13
  489.0 0.6 compare_reduce_fusion
  489.7 0.7 fusion.3
  490.3 4.9 custom-call.11
  495.2 0.3 convolution_bitcast_fusion
  495.6 0.0 copy-start.2
  495.6 2.1 fusion.25
  497.7 0.0 copy-done.2
  (8 shorter events, 0.2 us)
Async XLA Ops:
  7.2 325.7 %copy-start = (f32[512,64]{0,1:T(8,128)S(1)}, f32[512,64]{0,1:T(8,128)}, u32[]{:S(2)}) copy-start(f32[512,64]{0,1:T(8,128)} %param.6) | copy-start | bytes 393220
  7.2 325.6 %all-reduce.3.cloned.1.call-start = ((), (), s32[]{:S(2)}) async-start(), calls=%async_computation.1 | async-start | bytes 2097152 | tf_op jit(solution)/shard_map/psum | solution.py:26
  130.8 321.7 %all-reduce.5.cloned.1.call-start = ((), (), s32[]{:S(2)}) async-start(), calls=%async_computation.2 | async-start | bytes 2097152 | tf_op jit(solution)/shard_map/psum | solution.py:27
  452.5 15.2 %copy-start.1 = (f32[512,512]{1,0:T(8,128)S(1)}, f32[512,512]{1,0:T(8,128)}, u32[]{:S(2)}) copy-start(f32[512,512]{1,0:T(8,128)} %all-reduce.5.cloned.1.call-done) | copy-start | bytes 3145732
  495.6 2.1 copy-start.2
Sparse Core Ops, SparseCore 0:
  130.9 201.8 all-reduce.2
  336.4 116.0 all-reduce.4
